TPU v7x, 256 devices: a whole 4x4x8 slice. The times are simulated.
256 devices in a mesh: seq: 32 (over x, z), exp: 8 (over y, core).
Axes of the slice: x: 4, y: 4, z: 8, core: 2. Of those that a mesh axis runs over, the one named last changes fastest.
Arguments:
- queries: bfloat16 [32768, 4096], P(('seq', 'exp')), may hold values from -1.75 to 1.75
- keys: bfloat16 [32768, 4096], P(('seq', 'exp')), may hold values from -1.75 to 1.75
- values: bfloat16 [32768, 4096], P(('seq', 'exp')), may hold values from -6 to 6
- out_grad: bfloat16 [32768, 4096], P(('seq', 'exp')), may hold values from -0.0625 to 0.0625
- log_decay: bfloat16 [32768, 32], P(('seq', 'exp')), may hold values from -0.7 to 0
Outputs:
- query_grad: bfloat16 [32768, 4096], P(('seq', 'exp'))
- key_grad: bfloat16 [32768, 4096], P(('seq', 'exp'))
- value_grad: bfloat16 [32768, 4096], P(('seq', 'exp'))
All inputs are finite; a program needn't handle non-finite values.
Results may differ from a plain program's by a relative error of at most 0.0095.
Values may be sent and summed in bfloat16 or wider, within the bound.
No kernel may reach another device: no remote copies, remote signals or barrier semaphores. Data moves between devices by JAX's collectives and lax.ppermute only.
A program may use at most 64 MiB of HBM per device.

v0:
```python
import jax
import jax.numpy as jnp
from jax import lax
from jax.sharding import Mesh
from jax.sharding import PartitionSpec as P

BLOCK = 128
SEQ = ("seq_0", "seq_1")
SEQ_EXP = ("seq_0", "seq_1", "exp")


def filled_with(x, identity):
    return jax.tree.map(
        lambda part, zero: jnp.zeros_like(part) + jnp.asarray(zero, part.dtype), x, identity
    )


def carried_in(x, axes, combine, identity, reverse):
    before = start = filled_with(x, identity)
    total = x
    for axis in reversed(axes):
        peers, here = (lax.axis_size(axis), lax.axis_index(axis))
        pieces = jax.tree.map(lambda part: lax.all_gather(part, axis), total)
        inside, total = (start, start)
        for k in reversed(range(peers)) if reverse else range(peers):
            passed = k > here if reverse else k < here
            total = combine(total, jax.tree.map(lambda part: part[k], pieces))
            inside = jax.tree.map(lambda new, old: jnp.where(passed, new, old), total, inside)
        before = combine(inside, before)
    return before


def widen(array):
    return array.astype(jnp.float32)


def halves(array):
    high = array.astype(jnp.bfloat16)
    low = (array - widen(high)).astype(jnp.bfloat16)
    return (high, low)


def product(form, first_op, second_op):
    return jnp.einsum(form, first_op, second_op, preferred_element_type=jnp.float32)


def split_left(form, wide_op, narrow_op):
    high, low = halves(wide_op)
    return product(form, high, narrow_op) + product(form, low, narrow_op)


def split_right(form, narrow_op, wide_op):
    high, low = halves(wide_op)
    return product(form, narrow_op, high) + product(form, narrow_op, low)


def link(earlier, later):
    return (earlier[0] + later[0], jnp.exp(later[0])[:, None, None] * earlier[1] + later[1])


def key_side(key_loc, value_loc, decay_loc):
    rows = key_loc.shape[0]
    heads = decay_loc.shape[1]
    width = key_loc.shape[1] // heads
    blocks = rows // BLOCK
    key_blk = key_loc.reshape(blocks, BLOCK, heads, width)
    value_blk = value_loc.reshape(blocks, BLOCK, heads, width)
    cumul = jnp.cumsum(widen(decay_loc).reshape(blocks, BLOCK, heads), axis=1)
    totals = cumul[:, -1, :]
    after = jnp.exp(totals[:, None, :] - cumul)
    contrib = split_left("nsha,nshb->nhab", after[..., None] * widen(key_blk), value_blk)

    def key_step(carry, item):
        state, logsum = carry
        total, piece = item
        return ((jnp.exp(total)[:, None, None] * state + piece, logsum + total), (state, logsum))

    zero_state = jnp.zeros((heads, width, width), jnp.float32)
    zero_log = jnp.zeros((heads,), jnp.float32)
    (dev_state, dev_log), (prefix, prefix_log) = lax.scan(
        key_step, (zero_state, zero_log), (totals, contrib)
    )
    return (key_blk, value_blk, cumul, totals, after, prefix, prefix_log, dev_state, dev_log)


def query_side(query_loc, grad_loc, cumul, totals):
    blocks, length, heads = cumul.shape
    width = query_loc.shape[1] // heads
    query_blk = query_loc.reshape(blocks, length, heads, width)
    grad_blk = grad_loc.reshape(blocks, length, heads, width)
    before = jnp.exp(cumul)
    updates = split_left("ntha,nthb->nhab", before[..., None] * widen(query_blk), grad_blk)

    def query_step(carry, item):
        adjoint, logsum = carry
        total, piece = item
        return (
            (jnp.exp(total)[:, None, None] * adjoint + piece, logsum + total),
            (adjoint, logsum),
        )

    zero_state = jnp.zeros((heads, width, width), jnp.float32)
    zero_log = jnp.zeros((heads,), jnp.float32)
    (dev_adjoint, unused), (suffix, suffix_log) = lax.scan(
        query_step, (zero_state, zero_log), (totals, updates), reverse=True
    )
    return (query_blk, grad_blk, before, suffix, suffix_log, dev_adjoint)


def finish(
    query_blk,
    key_blk,
    value_blk,
    grad_blk,
    cumul,
    after,
    before,
    prefix,
    prefix_log,
    suffix,
    suffix_log,
    start_state,
    start_adjoint,
):
    state_prev = jnp.exp(prefix_log)[:, :, None, None] * start_state[None] + prefix
    adjoint = jnp.exp(suffix_log)[:, :, None, None] * start_adjoint[None] + suffix
    blocks, length, heads = cumul.shape
    width = key_blk.shape[3]
    heads_first = jnp.transpose(cumul, (0, 2, 1))
    spread = heads_first[:, :, :, None] - heads_first[:, :, None, :]
    causal = lax.broadcasted_iota(jnp.int32, (length, length), 1) <= lax.broadcasted_iota(
        jnp.int32, (length, length), 0
    )
    weights = jnp.where(
        causal[None, None], jnp.exp(jnp.where(causal[None, None], spread, 0.0)), 0.0
    )
    grad_scores = product("nthd,nshd->nhts", grad_blk, value_blk)
    key_scores = product("nthd,nshd->nhts", query_blk, key_blk)
    first = (weights * grad_scores).astype(jnp.bfloat16)
    second = (weights * key_scores).astype(jnp.bfloat16)
    query_part = product("nhts,nshd->nthd", first, key_blk)
    key_part = product("nhts,nthd->nshd", first, query_blk)
    value_part = product("nhts,nthd->nshd", second, grad_blk)
    grad_query = query_part + before[..., None] * split_right(
        "nthb,nhab->ntha", grad_blk, state_prev
    )
    adj_high, adj_low = halves(adjoint)
    grad_key = key_part + after[..., None] * (
        product("nshb,nhab->nsha", value_blk, adj_high)
        + product("nshb,nhab->nsha", value_blk, adj_low)
    )
    grad_value = value_part + after[..., None] * (
        product("nsha,nhab->nshb", key_blk, adj_high) + product("nsha,nhab->nshb", key_blk, adj_low)
    )
    rows = blocks * length
    flat_query = grad_query.astype(jnp.bfloat16).reshape(rows, heads * width)
    flat_key = grad_key.astype(jnp.bfloat16).reshape(rows, heads * width)
    flat_value = grad_value.astype(jnp.bfloat16).reshape(rows, heads * width)
    return (flat_query, flat_key, flat_value)


def body(queries, keys, values, out_grad, log_decay):
    query_loc, key_loc, value_loc, grad_loc, decay_loc = (
        lax.all_to_all(queries, "exp", split_axis=1, concat_axis=0, tiled=True),
        lax.all_to_all(keys, "exp", split_axis=1, concat_axis=0, tiled=True),
        lax.all_to_all(values, "exp", split_axis=1, concat_axis=0, tiled=True),
        lax.all_to_all(out_grad, "exp", split_axis=1, concat_axis=0, tiled=True),
        lax.all_to_all(log_decay, "exp", split_axis=1, concat_axis=0, tiled=True),
    )
    key_blk, value_blk, cumul, totals, after, prefix, prefix_log, dev_state, dev_log = key_side(
        key_loc, value_loc, decay_loc
    )
    heads = cumul.shape[2]
    width = key_blk.shape[3]
    zero_state = jnp.zeros((heads, width, width), jnp.float32)
    zero_log = jnp.zeros((heads,), jnp.float32)
    start_state = carried_in((dev_log, dev_state), SEQ, link, (zero_log, zero_state), False)[1]
    query_blk, grad_blk, before, suffix, suffix_log, dev_adjoint = query_side(
        query_loc, grad_loc, cumul, totals
    )
    start_adjoint = carried_in((dev_log, dev_adjoint), SEQ, link, (zero_log, zero_state), True)[1]
    flat_query, flat_key, flat_value = finish(
        query_blk,
        key_blk,
        value_blk,
        grad_blk,
        cumul,
        after,
        before,
        prefix,
        prefix_log,
        suffix,
        suffix_log,
        start_state,
        start_adjoint,
    )
    result = (
        lax.all_to_all(flat_query, "exp", split_axis=0, concat_axis=1, tiled=True),
        lax.all_to_all(flat_key, "exp", split_axis=0, concat_axis=1, tiled=True),
        lax.all_to_all(flat_value, "exp", split_axis=0, concat_axis=1, tiled=True),
    )
    return result


def solution(mesh):
    torus = Mesh(mesh.devices.reshape(4, 8, mesh.shape["exp"]), ("seq_0", "seq_1", "exp"))
    placed = (
        P(SEQ_EXP, None),
        P(SEQ_EXP, None),
        P(SEQ_EXP, None),
        P(SEQ_EXP, None),
        P(SEQ_EXP, None),
    )
    return jax.shard_map(
        body,
        mesh=torus,
        in_specs=placed,
        out_specs=(P(SEQ_EXP, None), P(SEQ_EXP, None), P(SEQ_EXP, None)),
        check_vma=False,
    )
```

profile of v0, /device:TPU:1, one launch (start us, length us, event | category | flops | bytes accessed | tf_op | source)
XLA Modules:
  0.0 307.2 jit_solution(12512901773788062015)
XLA Ops:
  7.2 6.5 %all-to-all-start = ((bf16[128,8,4]{0,2,1:T(4,128)(2,1)}), bf16[128,8,4]{0,2,1:T(4,128)(2,1)S(1)}, u32[]{:S(2)}, u32[]{:S(2)}) async-start(bf16[128,8,4]{0,2,1:T(4,128)(2,1)} %bitcast.362), calls=%async_computation | async-start | bytes 16384 | tf_op jit(solution)/shard_map/all_to_all | solution.py:168
  13.7 2.3 copy.61
  16.0 2.3 all-to-all-done
  18.3 4.2 %all-to-all-start.2 = ((bf16[128,8,512]{0,2,1:T(8,128)(2,1)}), bf16[128,8,512]{0,2,1:T(8,128)(2,1)S(1)}, u32[]{:S(2)}, u32[]{:S(2)}) async-start(bf16[128,8,512]{0,2,1:T(8,128)(2,1)} %bitcast.6), calls=%async_computation.2 | async-start | bytes 2097152 | tf_op jit(solution)/shard_map/all_to_all | solution.py:166
  22.5 1.3 copy.105
  23.8 13.8 %all-to-all-done.2 = bf16[128,8,512]{0,2,1:T(8,128)(2,1)S(1)} async-done(((bf16[128,8,512]{0,2,1:T(8,128)(2,1)}), bf16[128,8,512]{0,2,1:T(8,128)(2,1)S(1)}, u32[]{:S(2)}, u32[]{:S(2)}) %all-to-all-start.2) | async-done | bytes 1048608 | tf_op jit(solution)/shard_map/all_to_all | solution.py:166
  38.5 4.3 %all-to-all-start.3 = ((bf16[128,8,512]{0,2,1:T(8,128)(2,1)}), bf16[128,8,512]{0,2,1:T(8,128)(2,1)S(1)}, u32[]{:S(2)}, u32[]{:S(2)}) async-start(bf16[128,8,512]{0,2,1:T(8,128)(2,1)} %bitcast.9), calls=%async_computation.3 | async-start | bytes 2097152 | tf_op jit(solution)/shard_map/all_to_all | solution.py:165
  42.9 1.3 copy.60
  44.2 2.3 copy.107
  46.7 23.3 %fusion.89 = f32[8,128,4]{2,0,1:T(8,128)S(1)} fusion(f32[8,128,4]{2,0,1:T(8,128)S(1)} %copy.57), kind=kOutput, calls=%fused_computation.176 | output fusion | flops 520192 | bytes 32768 | tf_op jit(solution)/shard_map/jit(cumsum)/reduce_window_sum | solution.py:68
  70.2 4.8 %all-to-all-start.1 = ((bf16[128,8,512]{0,2,1:T(8,128)(2,1)}), bf16[128,8,512]{0,2,1:T(8,128)(2,1)S(1)}, u32[]{:S(2)}, u32[]{:S(2)}) async-start(bf16[128,8,512]{0,2,1:T(8,128)(2,1)} %bitcast.358), calls=%async_computation.1 | async-start | bytes 2097152 | tf_op jit(solution)/shard_map/all_to_all | solution.py:167
  75.0 1.1 fusion.88
  76.2 1.2 copy.68
  77.4 1.2 copy.65
  78.6 2.2 fusion.18
  80.8 2.2 convolution_add_fusion.1
  83.0 7.1 %all-to-all-done.1 = bf16[128,8,512]{0,2,1:T(8,128)(2,1)S(1)} async-done(((bf16[128,8,512]{0,2,1:T(8,128)(2,1)}), bf16[128,8,512]{0,2,1:T(8,128)(2,1)S(1)}, u32[]{:S(2)}, u32[]{:S(2)}) %all-to-all-start.1) | async-done | bytes 1048608 | tf_op jit(solution)/shard_map/all_to_all | solution.py:167
  90.1 5.0 %all-to-all-start.5 = ((bf16[128,8,512]{0,2,1:T(8,128)(2,1)}), bf16[128,8,512]{0,2,1:T(8,128)(2,1)}, u32[]{:S(2)}, u32[]{:S(2)}) async-start(bf16[128,8,512]{0,2,1:T(8,128)(2,1)} %bitcast.357), calls=%async_computation.5 | async-start | bytes 2097152 | tf_op jit(solution)/shard_map/all_to_all | solution.py:164
  95.1 1.6 broadcast_in_dim.43.clone
  96.8 14.8 %while.38 = (s32[]{:T(128)}, f32[4,128,128]{2,1,0:T(8,128)S(1)}, f32[4]{0:T(128)S(1)}, f32[8,4,128,128]{3,2,1,0:T(8,128)}, f32[8,4]{1,0:T(8,128)S(1)}, /*index=5...) while((s32[]{:T(128)}, f32[4,128,128]{2,1,0:T(8,128)S(1)}, ...), condition=%wide.region_2.3_spmd.clone, body=%wide.region_1.2_spmd.clone.sunk | while | flops 262155 | bytes 1310977 | solution.py:80
  97.5 1.0 bitcast_add_fusion.13
  99.4 1.0 bitcast_add_fusion.13
  101.2 1.0 bitcast_add_fusion.13
  103.0 1.0 bitcast_add_fusion.13
  104.9 1.0 bitcast_add_fusion.13
  112.4 2.1 fusion.20
  114.4 3.4 %convolution_add_fusion = f32[8,4,128,128]{3,2,1,0:T(8,128)} fusion(f32[8,4,128,128]{3,2,1,0:T(8,128)S(1)} %fusion.20, bf16[8,128,4,128]{1,3,2,0:T(8,128)(2,1)S(1)} %bitcast.345, bf16[8,128,4,128]{1,3,2,0:T(8,128)(2,1)} %bitcast.46, f32[8,128,4]{1,2,0:T(4,128)S(1)} %copy.65), kind=kOutput, calls=%fused_computation.40 | convolution fusion | flops 137887744 | bytes 6307840 | tf_op jit(solution)/shard_map/ntha,nthb->nhab/dot_general | solution.py:44
  118.1 9.3 %while.39 = (s32[]{:T(128)}, f32[4,128,128]{2,1,0:T(8,128)S(1)}, f32[4]{0:T(128)S(1)}, f32[8,4,128,128]{3,2,1,0:T(8,128)S(1)}, f32[8,4]{1,0:T(8,128)S(1)}, /*ind...) while((s32[]{:T(128)}, f32[4,128,128]{2,1,0:T(8,128)S(1)}, ...), condition=%wide.region_4.5_spmd.clone, body=%wide.region_3.4_spmd.clone.sunk | while | flops 262156 | bytes 1310997 | solution.py:104
  118.2 1.0 bitcast_add_fusion.14
  119.3 1.0 bitcast_add_fusion.14
  120.5 1.0 bitcast_add_fusion.14
  121.6 1.0 bitcast_add_fusion.14
  122.8 1.0 bitcast_add_fusion.14
  124.0 1.0 bitcast_add_fusion.14
  125.1 1.0 bitcast_add_fusion.14
  126.3 1.0 bitcast_add_fusion.14
  129.6 16.9 %all-reduce = f32[32]{0:T(128)S(1)} all-reduce(f32[32]{0:T(128)S(1)} %dynamic-update-slice), channel_id=2, replica_groups=mesh['seq_0'=4,'seq_1'=8,'exp'=8] {'seq_1'}, use_global_device_ids=true, to_apply=%add | all-reduce | flops 32 | bytes 256
  146.8 5.6 %all-gather.14.cloned.1.call-done = f32[32,128,128]{2,1,0:T(8,128)} async-done(((f32[4,128,128]{2,1,0:T(8,128)}), f32[32,128,128]{2,1,0:T(8,128)}) %all-gather.14.cloned.1.call-update) | async-done | bytes 2097168 | tf_op jit(solution)/shard_map/all_gather | solution.py:23
  152.4 2.5 fusion.56
  155.0 1.2 copy.58
  156.3 7.4 %all-gather.3 = f32[4,1,4]{2,1,0:T(1,128)S(1)} all-gather(f32[1,1,4]{2,1,0:T(1,128)S(1)} %get-tuple-element.336), channel_id=1, replica_groups=mesh['seq_0'=4,'seq_1'=8,'exp'=8] {'seq_0'}, dimensions={0}, use_global_device_ids=true | all-gather | bytes 80 | tf_op jit(solution)/shard_map/all_gather | solution.py:23
  163.7 5.2 %all-gather.4 = f32[4,1,4]{2,1,0:T(1,128)S(1)} all-gather(f32[1,1,4]{2,1,0:T(1,128)S(1)} %get-tuple-element.335), channel_id=1, replica_groups=mesh['seq_0'=4,'seq_1'=8,'exp'=8] {'seq_0'}, dimensions={0}, use_global_device_ids=true | all-gather | bytes 80 | tf_op jit(solution)/shard_map/all_gather | solution.py:23
  168.9 3.5 %multiply_convert_fusion.1 = bf16[8,4,128,128]{3,2,1,0:T(8,128)(2,1)} fusion(bf16[8,128,4,128]{1,3,2,0:T(8,128)(2,1)} %bitcast.346, bf16[8,128,4,128]{1,3,2,0:T(8,128)(2,1)} %bitcast.351, f32[8,4,128]{2,1,0:T(4,128)S(1)} %copy.58, pred[128,128]{1,0:T(8,128)(4,1)S(1)} %iota_compare_fusion), kind=kOutput, calls=%fused_computation.36 | convolution fusion | flops 136839168 | bytes 3178496 | tf_op jit(solution)/shard_map/nthd,nshd->nhts/dot_general | solution.py:44
  172.4 21.3 %all-gather.16.cloned.1.call-done = f32[32,128,128]{2,1,0:T(8,128)} async-done(((f32[4,128,128]{2,1,0:T(8,128)}), f32[32,128,128]{2,1,0:T(8,128)}) %all-gather.16.cloned.1.call-update) | async-done | bytes 2097168 | tf_op jit(solution)/shard_map/all_gather | solution.py:23
  193.7 2.4 fusion.44
  196.2 3.5 %fusion.90 = f32[8,4,128,128]{2,3,1,0:T(8,128)} fusion(bf16[8,4,128,128]{3,2,1,0:T(8,128)(2,1)} %multiply_convert_fusion.1, bf16[8,128,4,128]{1,3,2,0:T(8,128)(2,1)S(1)} %bitcast.340), kind=kOutput, calls=%fused_computation.177 | convolution fusion | flops 134217728 | bytes 4194304 | tf_op jit(solution)/shard_map/nhts,nshd->nthd/dot_general | solution.py:44
  199.7 23.7 %all-gather.10.cloned.1.call-done = f32[4,4,128,128]{3,2,1,0:T(8,128)} async-done(((f32[1,4,128,128]{3,2,1,0:T(8,128)}), f32[4,4,128,128]{3,2,1,0:T(8,128)}) %all-gather.10.cloned.1.call-update) | async-done | bytes 1048592 | tf_op jit(solution)/shard_map/all_gather | solution.py:23
  223.4 2.4 fusion.55
  226.7 1.1 copy-done.8
  227.8 1.7 fusion.13
  229.5 5.9 %all-to-all-start.4 = ((bf16[8,128,512]{1,2,0:T(8,128)(2,1)}), bf16[8,128,512]{1,2,0:T(8,128)(2,1)}, u32[]{:S(2)}, u32[]{:S(2)}) async-start(bf16[8,128,512]{1,2,0:T(8,128)(2,1)} %bitcast.360), calls=%async_computation.4 | async-start | bytes 2097152 | tf_op jit(solution)/shard_map/all_to_all | solution.py:198
  235.3 16.6 %all-gather.12.cloned.1.call-done = f32[4,4,128,128]{3,2,1,0:T(8,128)} async-done(((f32[1,4,128,128]{3,2,1,0:T(8,128)}), f32[4,4,128,128]{3,2,1,0:T(8,128)}) %all-gather.12.cloned.1.call-update) | async-done | bytes 1048592 | tf_op jit(solution)/shard_map/all_gather | solution.py:23
  251.9 2.3 fusion.43
  256.0 2.8 fusion.11
  258.8 5.9 %all-to-all-start.6 = ((bf16[8,128,512]{1,2,0:T(8,128)(2,1)}), bf16[8,128,512]{1,2,0:T(8,128)(2,1)}, u32[]{:S(2)}, u32[]{:S(2)}) async-start(bf16[8,128,512]{1,2,0:T(8,128)(2,1)} %bitcast.356), calls=%async_computation.6 | async-start | bytes 2097152 | tf_op jit(solution)/shard_map/all_to_all | solution.py:199
  264.7 2.1 fusion.36
  266.8 2.1 fusion.84
  268.9 5.1 %fusion.9 = bf16[8,128,4,128]{1,3,2,0:T(8,128)(2,1)} fusion(f32[8,4,128,128]{3,2,1,0:T(8,128)} %fusion.36, f32[8,4,128,128]{3,2,1,0:T(8,128)} %fusion.84, bf16[8,128,4,128]{1,3,2,0:T(8,128)(2,1)} %bitcast.347, bf16[8,128,4,128]{1,3,2,0:T(8,128)(2,1)} %bitcast.46, bf16[8,128,4,128]{1,3,2,0:T(8,128)(2,1)S(1)} %bitcast.343, f32[8,128,4]{1,2,0:T(4,128)S(1)} %copy.68, ...), kind=kOutput, calls=%fused_computation.18 | convolution fusion | flops 273154048 | bytes 8437760 | tf_op jit(solution)/shard_map/nhts,nthd->nshd/dot_general | solution.py:44
  274.0 5.9 %all-to-all-done.6 = bf16[8,128,512]{1,2,0:T(8,128)(2,1)} async-done(((bf16[8,128,512]{1,2,0:T(8,128)(2,1)}), bf16[8,128,512]{1,2,0:T(8,128)(2,1)}, u32[]{:S(2)}, u32[]{:S(2)}) %all-to-all-start.6) | async-done | bytes 1048608 | tf_op jit(solution)/shard_map/all_to_all | solution.py:199
  279.9 4.3 %all-to-all-start.7 = ((bf16[8,128,512]{1,2,0:T(8,128)(2,1)}), bf16[8,128,512]{1,2,0:T(8,128)(2,1)S(1)}, u32[]{:S(2)}, u32[]{:S(2)}) async-start(bf16[8,128,512]{1,2,0:T(8,128)(2,1)} %bitcast.69), calls=%async_computation.7 | async-start | bytes 2097152 | tf_op jit(solution)/shard_map/all_to_all | solution.py:200
  284.2 2.3 copy.106
  286.5 2.3 copy.108
  288.7 10.6 %all-to-all-done.7 = bf16[8,128,512]{1,2,0:T(8,128)(2,1)S(1)} async-done(((bf16[8,128,512]{1,2,0:T(8,128)(2,1)}), bf16[8,128,512]{1,2,0:T(8,128)(2,1)S(1)}, u32[]{:S(2)}, u32[]{:S(2)}) %all-to-all-start.7) | async-done | bytes 1048608 | tf_op jit(solution)/shard_map/all_to_all | solution.py:200
  299.3 1.3 copy.109
  (118 shorter events, 17.1 us)
Async XLA Ops:
  7.2 11.1 %all-to-all-start = ((bf16[128,8,4]{0,2,1:T(4,128)(2,1)}), bf16[128,8,4]{0,2,1:T(4,128)(2,1)S(1)}, u32[]{:S(2)}, u32[]{:S(2)}) async-start(bf16[128,8,4]{0,2,1:T(4,128)(2,1)} %bitcast.362), calls=%async_computation | async-start | bytes 16384 | tf_op jit(solution)/shard_map/all_to_all | solution.py:168
  13.6 8.8 %copy-start.12 = (bf16[128,4096]{1,0:T(8,128)(2,1)S(1)}, bf16[128,4096]{1,0:T(8,128)(2,1)}, u32[]{:S(2)}) copy-start(bf16[128,4096]{1,0:T(8,128)(2,1)} %param.10) | copy-start | bytes 3145732
  18.3 19.3 %all-to-all-start.2 = ((bf16[128,8,512]{0,2,1:T(8,128)(2,1)}), bf16[128,8,512]{0,2,1:T(8,128)(2,1)S(1)}, u32[]{:S(2)}, u32[]{:S(2)}) async-start(bf16[128,8,512]{0,2,1:T(8,128)(2,1)} %bitcast.6), calls=%async_computation.2 | async-start | bytes 2097152 | tf_op jit(solution)/shard_map/all_to_all | solution.py:166
  22.4 20.4 %copy-start.13 = (bf16[128,4096]{1,0:T(8,128)(2,1)S(1)}, bf16[128,4096]{1,0:T(8,128)(2,1)}, u32[]{:S(2)}) copy-start(bf16[128,4096]{1,0:T(8,128)(2,1)} %param.12) | copy-start | bytes 3145732
  37.6 1.0 copy-start.4
  38.5 31.7 %all-to-all-start.3 = ((bf16[128,8,512]{0,2,1:T(8,128)(2,1)}), bf16[128,8,512]{0,2,1:T(8,128)(2,1)S(1)}, u32[]{:S(2)}, u32[]{:S(2)}) async-start(bf16[128,8,512]{0,2,1:T(8,128)(2,1)} %bitcast.9), calls=%async_computation.3 | async-start | bytes 2097152 | tf_op jit(solution)/shard_map/all_to_all | solution.py:165
  70.0 7.4 %copy-start.9 = (f32[8,128,4]{2,0,1:T(8,128)}, f32[8,128,4]{2,0,1:T(8,128)S(1)}, u32[]{:S(2)}) copy-start(f32[8,128,4]{2,0,1:T(8,128)S(1)} %fusion.89) | copy-start | bytes 49156
  70.2 19.9 %all-to-all-start.1 = ((bf16[128,8,512]{0,2,1:T(8,128)(2,1)}), bf16[128,8,512]{0,2,1:T(8,128)(2,1)S(1)}, u32[]{:S(2)}, u32[]{:S(2)}) async-start(bf16[128,8,512]{0,2,1:T(8,128)(2,1)} %bitcast.358), calls=%async_computation.1 | async-start | bytes 2097152 | tf_op jit(solution)/shard_map/all_to_all | solution.py:167
  78.6 2.2 copy-start.5
  90.1 24.3 %copy-start = (bf16[128,8,512]{0,2,1:T(8,128)(2,1)}, bf16[128,8,512]{0,2,1:T(8,128)(2,1)S(1)}, u32[]{:S(2)}) copy-start(bf16[128,8,512]{0,2,1:T(8,128)(2,1)S(1)} %all-to-all-done.1) | copy-start | bytes 3145732
  90.1 22.2 %all-to-all-start.5 = ((bf16[128,8,512]{0,2,1:T(8,128)(2,1)}), bf16[128,8,512]{0,2,1:T(8,128)(2,1)}, u32[]{:S(2)}, u32[]{:S(2)}) async-start(bf16[128,8,512]{0,2,1:T(8,128)(2,1)} %bitcast.357), calls=%async_computation.5 | async-start | bytes 2097152 | tf_op jit(solution)/shard_map/all_to_all | solution.py:164
  95.1 57.2 %all-gather.14.cloned.1.call-start = ((), (), s32[]{:S(2)}) async-start(), calls=%async_computation.10 | async-start | bytes 2359296 | tf_op jit(solution)/shard_map/all_gather | solution.py:23
  111.6 0.7 copy-start.3
  112.3 81.4 %all-gather.16.cloned.1.call-start = ((), (), s32[]{:S(2)}) async-start(), calls=%async_computation.11 | async-start | bytes 2359296 | tf_op jit(solution)/shard_map/all_gather | solution.py:23
  118.1 10.1 %copy-start.14 = (u32[256]{0:T(256)S(1)}, u32[256]{0:T(256)}, u32[]{:S(2)}) copy-start(u32[256]{0:T(256)} %constant.92) | copy-start | bytes 3076
  127.4 0.7 copy-start.2
  128.1 95.3 %all-gather.10.cloned.1.call-start = ((), (), s32[]{:S(2)}) async-start(), calls=%async_computation.8 | async-start | bytes 1310720 | tf_op jit(solution)/shard_map/all_gather | solution.py:23
  154.9 97.0 %all-gather.12.cloned.1.call-start = ((), (), s32[]{:S(2)}) async-start(), calls=%async_computation.9 | async-start | bytes 1310720 | tf_op jit(solution)/shard_map/all_gather | solution.py:23
  196.2 27.2 %copy-start.11 = (f32[1,4,128,128]{3,2,1,0:T(8,128)S(1)}, f32[1,4,128,128]{3,2,1,0:T(8,128)}, u32[]{:S(2)}) copy-start(f32[1,4,128,128]{3,2,1,0:T(8,128)} %get-tuple-element.313) | copy-start | bytes 786436
  223.4 2.4 copy-start.1
  223.4 2.8 copy-start.7
  226.2 1.6 copy-start.8
  229.5 29.3 %all-to-all-start.4 = ((bf16[8,128,512]{1,2,0:T(8,128)(2,1)}), bf16[8,128,512]{1,2,0:T(8,128)(2,1)}, u32[]{:S(2)}, u32[]{:S(2)}) async-start(bf16[8,128,512]{1,2,0:T(8,128)(2,1)} %bitcast.360), calls=%async_computation.4 | async-start | bytes 2097152 | tf_op jit(solution)/shard_map/all_to_all | solution.py:198
  251.9 2.3 copy-start.6
  254.8 1.2 copy-start.10
  258.8 21.1 %all-to-all-start.6 = ((bf16[8,128,512]{1,2,0:T(8,128)(2,1)}), bf16[8,128,512]{1,2,0:T(8,128)(2,1)}, u32[]{:S(2)}, u32[]{:S(2)}) async-start(bf16[8,128,512]{1,2,0:T(8,128)(2,1)} %bitcast.356), calls=%async_computation.6 | async-start | bytes 2097152 | tf_op jit(solution)/shard_map/all_to_all | solution.py:199
  279.9 19.4 %all-to-all-start.7 = ((bf16[8,128,512]{1,2,0:T(8,128)(2,1)}), bf16[8,128,512]{1,2,0:T(8,128)(2,1)S(1)}, u32[]{:S(2)}, u32[]{:S(2)}) async-start(bf16[8,128,512]{1,2,0:T(8,128)(2,1)} %bitcast.69), calls=%async_computation.7 | async-start | bytes 2097152 | tf_op jit(solution)/shard_map/all_to_all | solution.py:200
Sparse Core Ops, SparseCore 0:
  112.4 39.9 all-gather.13
  154.2 39.4 all-gather.15
  195.5 27.8 all-gather.9
  225.1 26.8 all-gather.11
where the time goes:
time: 309 us; the launch traced here: 307 us
  waiting for transfers between devices  107 us (35%)
  other arithmetic  57.4 us (19%)
  starting transfers between devices  41 us (13%)
  matrix products  32.2 us (10%)
  blocking collectives  29.5 us (10%)
  local copies, waits for them, and re-layouts  25.1 us (8%)
  between operations  14.7 us (5%)
    all_gather x4, waiting for transfers between devices, carried_in(): pieces = jax.tree.map(lambda part: lax.all_gather(part, axis), total)  67.3 us
    dot_general x14, matrix products, product(): jnp.einsum(form, first_op, second_op, preferred_element_type=jnp.float32)  32.2 us
    another operation x1, other arithmetic, key_side(): cumul = jnp.cumsum(widen(decay_loc).reshape(blocks, BLOCK, heads), axis=1)  23.3 us
    unnamed x1, blocking collectives  16.9 us
    all_to_all x1, waiting for transfers between devices, body(): lax.all_to_all(values, 'exp', split_axis=1, concat_axis=0, tiled=True)  13.8 us
    all_gather x2, blocking collectives, carried_in(): pieces = jax.tree.map(lambda part: lax.all_gather(part, axis), total)  12.5 us
    all_to_all x1, waiting for transfers between devices, body(): lax.all_to_all(flat_value, 'exp', split_axis=0, concat_axis=1, tiled=True)  10.6 us
    unnamed x36, local copies, waits for them, and re-layouts  9.1 us
  transfers between devices with their start and end apart: 12, of which 9 were waited for; matrix products, arithmetic and copies ran while one was open for 35% of the time, Pallas kernels for 0%

commit v1 on v0

--- a/solution.py
+++ b/solution.py
@@ -7,6 +7,15 @@
 BLOCK = 128
 SEQ = ("seq_0", "seq_1")
 SEQ_EXP = ("seq_0", "seq_1", "exp")
+
+
+def lay_strings_over_axis(xx, ax_name):
+    return jnp.concatenate(
+        jax.lax.all_to_all(
+            jnp.stack(jnp.split(xx, jax.lax.axis_size(ax_name), axis=1)), ax_name, 0, 0
+        ),
+        axis=0,
+    )
 
 
 def filled_with(x, identity):
@@ -164,7 +173,7 @@
         lax.all_to_all(queries, "exp", split_axis=1, concat_axis=0, tiled=True),
         lax.all_to_all(keys, "exp", split_axis=1, concat_axis=0, tiled=True),
         lax.all_to_all(values, "exp", split_axis=1, concat_axis=0, tiled=True),
-        lax.all_to_all(out_grad, "exp", split_axis=1, concat_axis=0, tiled=True),
+        lay_strings_over_axis(out_grad, "exp"),
         lax.all_to_all(log_decay, "exp", split_axis=1, concat_axis=0, tiled=True),
     )
     key_blk, value_blk, cumul, totals, after, prefix, prefix_log, dev_state, dev_log = key_side(

time: 309 us -> 298 us (0.964)
  other arithmetic: 57.4 us -> 35.3 us
  waiting for transfers between devices: 107 us -> 118 us
    another operation x1, other arithmetic: 23.3 us -> 1.18 us  [key_side(): cumul = jnp.cumsum(widen(decay_loc).reshape(blocks, BLOCK, heads), axis=1)]
    all_to_all x1, waiting for transfers between devices: 0.01 us -> 11.4 us  [body(): lax.all_to_all(keys, 'exp', split_axis=1, concat_axis=0, tiled=True)]
    unnamed x36 -> x50, local copies, waits for them, and re-layouts: 9.1 us -> 7.26 us
  transfers between devices with their start and end apart: 12 -> 12, of which waited for: 9 -> 9; matrix products, arithmetic and copies ran while one was open for 35% -> 29% of each run, Pallas kernels for 0% -> 0%
where the time goes in v1:
time: 298 us; the launch traced here: 297 us
  waiting for transfers between devices  118 us (40%)
  starting transfers between devices  41.2 us (14%)
  other arithmetic  35.3 us (12%)
  blocking collectives  30.8 us (10%)
  matrix products  29.9 us (10%)
  local copies, waits for them, and re-layouts  26.2 us (9%)
  between operations  14.9 us (5%)
    all_gather x4, waiting for transfers between devices, carried_in(): pieces = jax.tree.map(lambda part: lax.all_gather(part, axis), total)  64.6 us
    dot_general x14, matrix products, product(): jnp.einsum(form, first_op, second_op, preferred_element_type=jnp.float32)  29.9 us
    unnamed x1, blocking collectives  17.3 us
    all_to_all x1, waiting for transfers between devices, body(): lax.all_to_all(values, 'exp', split_axis=1, concat_axis=0, tiled=True)  15 us
    all_gather x2, blocking collectives, carried_in(): pieces = jax.tree.map(lambda part: lax.all_gather(part, axis), total)  13.5 us
    all_to_all x1, waiting for transfers between devices, body(): lax.all_to_all(keys, 'exp', split_axis=1, concat_axis=0, tiled=True)  11.4 us
    all_to_all x1, waiting for transfers between devices, body(): lax.all_to_all(flat_value, 'exp', split_axis=0, concat_axis=1, tiled=True)  10.6 us
    all_to_all x1, waiting for transfers between devices, lay_strings_over_axis(): jax.lax.all_to_all(jnp.stack(jnp.split(xx, jax.lax.axis_size(ax_name), ax...  8.57 us
  transfers between devices with their start and end apart: 12, of which 9 were waited for; matrix products, arithmetic and copies ran while one was open for 29% of the time, Pallas kernels for 0%

profile of v1, /device:TPU:1, one launch (start us, length us, event | category | flops | bytes accessed | tf_op | source)
XLA Modules:
  0.0 296.6 jit_solution(7164270519263058525)
XLA Ops:
  7.2 6.5 %all-to-all-start = ((bf16[128,8,4]{0,2,1:T(4,128)(2,1)}), bf16[128,8,4]{0,2,1:T(4,128)(2,1)S(1)}, u32[]{:S(2)}, u32[]{:S(2)}) async-start(bf16[128,8,4]{0,2,1:T(4,128)(2,1)} %bitcast.374), calls=%async_computation | async-start | bytes 16384 | tf_op jit(solution)/shard_map/all_to_all | solution.py:177
  13.7 1.4 fusion.88
  16.2 1.3 copy.75
  17.5 2.3 copy.119
  19.9 1.3 copy.121
  21.2 4.8 %all-to-all-start.2 = ((bf16[128,8,512]{0,2,1:T(8,128)(2,1)}), bf16[128,8,512]{0,2,1:T(8,128)(2,1)S(1)}, u32[]{:S(2)}, u32[]{:S(2)}) async-start(bf16[128,8,512]{0,2,1:T(8,128)(2,1)} %bitcast.12), calls=%async_computation.2 | async-start | bytes 2097152 | tf_op jit(solution)/shard_map/all_to_all | solution.py:175
  26.1 15.0 %all-to-all-done.2 = bf16[128,8,512]{0,2,1:T(8,128)(2,1)S(1)} async-done(((bf16[128,8,512]{0,2,1:T(8,128)(2,1)}), bf16[128,8,512]{0,2,1:T(8,128)(2,1)S(1)}, u32[]{:S(2)}, u32[]{:S(2)}) %all-to-all-start.2) | async-done | bytes 1048608 | tf_op jit(solution)/shard_map/all_to_all | solution.py:175
  41.1 4.3 %all-to-all-start.3 = ((bf16[128,8,512]{0,2,1:T(8,128)(2,1)}), bf16[128,8,512]{0,2,1:T(8,128)(2,1)S(1)}, u32[]{:S(2)}, u32[]{:S(2)}) async-start(bf16[128,8,512]{0,2,1:T(8,128)(2,1)} %bitcast.369), calls=%async_computation.3 | async-start | bytes 2097152 | tf_op jit(solution)/shard_map/all_to_all | solution.py:174
  47.8 1.2 fusion.90
  49.2 11.4 %all-to-all-done.3 = bf16[128,8,512]{0,2,1:T(8,128)(2,1)S(1)} async-done(((bf16[128,8,512]{0,2,1:T(8,128)(2,1)}), bf16[128,8,512]{0,2,1:T(8,128)(2,1)S(1)}, u32[]{:S(2)}, u32[]{:S(2)}) %all-to-all-start.3) | async-done | bytes 1048608 | tf_op jit(solution)/shard_map/all_to_all | solution.py:174
  60.5 5.0 %all-to-all-start.1 = ((bf16[8,128,512]{1,2,0:T(8,128)(2,1)}), bf16[8,128,512]{1,2,0:T(8,128)(2,1)}, u32[]{:S(2)}, u32[]{:S(2)}) async-start(bf16[8,128,512]{1,2,0:T(8,128)(2,1)} %bitcast_dynamic-update-slice_fusion.2), calls=%async_computation.1 | async-start | bytes 2097152 | tf_op jit(solution)/shard_map/all_to_all | solution.py:14
  65.5 1.1 fusion.89
  66.7 1.2 copy.82
  67.9 1.2 copy.79
  70.0 2.2 convolution_add_fusion.1
  72.2 8.6 %all-to-all-done.1 = bf16[8,128,512]{1,2,0:T(8,128)(2,1)} async-done(((bf16[8,128,512]{1,2,0:T(8,128)(2,1)}), bf16[8,128,512]{1,2,0:T(8,128)(2,1)}, u32[]{:S(2)}, u32[]{:S(2)}) %all-to-all-start.1) | async-done | bytes 1048608 | tf_op jit(solution)/shard_map/all_to_all | solution.py:14
  80.8 4.3 %all-to-all-start.5 = ((bf16[128,8,512]{0,2,1:T(8,128)(2,1)}), bf16[128,8,512]{0,2,1:T(8,128)(2,1)S(1)}, u32[]{:S(2)}, u32[]{:S(2)}) async-start(bf16[128,8,512]{0,2,1:T(8,128)(2,1)} %bitcast.368), calls=%async_computation.5 | async-start | bytes 2097152 | tf_op jit(solution)/shard_map/all_to_all | solution.py:173
  85.1 1.6 broadcast_in_dim.43.clone
  86.7 14.8 %while.38 = (s32[]{:T(128)}, f32[4,128,128]{2,1,0:T(8,128)S(1)}, f32[4]{0:T(128)S(1)}, f32[8,4,128,128]{3,2,1,0:T(8,128)}, f32[8,4]{1,0:T(8,128)S(1)}, /*index=5...) while((s32[]{:T(128)}, f32[4,128,128]{2,1,0:T(8,128)S(1)}, ...), condition=%wide.region_2.3_spmd.clone, body=%wide.region_1.2_spmd.clone.sunk | while | flops 262155 | bytes 1310977 | solution.py:89
  87.5 1.0 bitcast_add_fusion.13
  89.3 1.0 bitcast_add_fusion.13
  91.2 1.0 bitcast_add_fusion.13
  93.0 1.0 bitcast_add_fusion.13
  94.9 1.0 bitcast_add_fusion.13
  96.7 1.0 bitcast_add_fusion.13
  98.6 1.0 bitcast_add_fusion.13
  102.3 2.4 fusion.20
  104.8 3.4 %convolution_add_fusion = f32[8,4,128,128]{3,2,1,0:T(8,128)} fusion(f32[8,4,128,128]{3,2,1,0:T(8,128)S(1)} %fusion.20, bf16[8,128,4,128]{1,3,2,0:T(8,128)(2,1)} %bitcast.11, bf16[8,128,4,128]{1,3,2,0:T(8,128)(2,1)S(1)} %bitcast.363, f32[8,128,4]{1,2,0:T(4,128)S(1)} %copy.79), kind=kOutput, calls=%fused_computation.40 | convolution fusion | flops 137887744 | bytes 6307840 | tf_op jit(solution)/shard_map/ntha,nthb->nhab/dot_general | solution.py:53
  108.5 9.3 %while.39 = (s32[]{:T(128)}, f32[4,128,128]{2,1,0:T(8,128)S(1)}, f32[4]{0:T(128)S(1)}, f32[8,4,128,128]{3,2,1,0:T(8,128)S(1)}, f32[8,4]{1,0:T(8,128)S(1)}, /*ind...) while((s32[]{:T(128)}, f32[4,128,128]{2,1,0:T(8,128)S(1)}, ...), condition=%wide.region_4.5_spmd.clone, body=%wide.region_3.4_spmd.clone.sunk | while | flops 262156 | bytes 1310997 | solution.py:113
  108.5 1.0 bitcast_add_fusion.14
  109.7 1.0 bitcast_add_fusion.14
  110.8 1.0 bitcast_add_fusion.14
  112.0 1.0 bitcast_add_fusion.14
  113.2 1.0 bitcast_add_fusion.14
  114.3 1.0 bitcast_add_fusion.14
  115.5 1.1 bitcast_add_fusion.14
  116.6 1.0 bitcast_add_fusion.14
  120.1 17.3 %all-reduce = f32[32]{0:T(128)S(1)} all-reduce(f32[32]{0:T(128)S(1)} %dynamic-update-slice), channel_id=2, replica_groups=mesh['seq_0'=4,'seq_1'=8,'exp'=8] {'seq_1'}, use_global_device_ids=true, to_apply=%add | all-reduce | flops 32 | bytes 256
  137.6 4.5 %all-gather.14.cloned.1.call-done = f32[32,128,128]{2,1,0:T(8,128)} async-done(((f32[4,128,128]{2,1,0:T(8,128)}), f32[32,128,128]{2,1,0:T(8,128)}) %all-gather.14.cloned.1.call-update) | async-done | bytes 2097168 | tf_op jit(solution)/shard_map/all_gather | solution.py:32
  142.1 2.4 fusion.57
  144.6 1.2 copy.65
  146.0 8.3 %all-gather.3 = f32[4,1,4]{2,1,0:T(1,128)S(1)} all-gather(f32[1,1,4]{2,1,0:T(1,128)S(1)} %get-tuple-element.344), channel_id=1, replica_groups=mesh['seq_0'=4,'seq_1'=8,'exp'=8] {'seq_0'}, dimensions={0}, use_global_device_ids=true | all-gather | bytes 80 | tf_op jit(solution)/shard_map/all_gather | solution.py:32
  154.2 5.2 %all-gather.4 = f32[4,1,4]{2,1,0:T(1,128)S(1)} all-gather(f32[1,1,4]{2,1,0:T(1,128)S(1)} %get-tuple-element.343), channel_id=1, replica_groups=mesh['seq_0'=4,'seq_1'=8,'exp'=8] {'seq_0'}, dimensions={0}, use_global_device_ids=true | all-gather | bytes 80 | tf_op jit(solution)/shard_map/all_gather | solution.py:32
  159.4 3.5 %multiply_convert_fusion.1 = bf16[8,4,128,128]{3,2,1,0:T(8,128)(2,1)} fusion(bf16[8,128,4,128]{1,3,2,0:T(8,128)(2,1)} %bitcast.11, bf16[8,128,4,128]{1,3,2,0:T(8,128)(2,1)} %bitcast.359, f32[8,4,128]{2,1,0:T(4,128)S(1)} %copy.65, pred[128,128]{1,0:T(8,128)(4,1)S(1)} %iota_compare_fusion), kind=kOutput, calls=%fused_computation.36 | convolution fusion | flops 136839168 | bytes 3178496 | tf_op jit(solution)/shard_map/nthd,nshd->nhts/dot_general | solution.py:53
  162.9 20.5 %all-gather.16.cloned.1.call-done = f32[32,128,128]{2,1,0:T(8,128)} async-done(((f32[4,128,128]{2,1,0:T(8,128)}), f32[32,128,128]{2,1,0:T(8,128)}) %all-gather.16.cloned.1.call-update) | async-done | bytes 2097168 | tf_op jit(solution)/shard_map/all_gather | solution.py:32
  183.5 2.5 fusion.45
  186.0 3.4 %fusion.91 = f32[8,4,128,128]{2,3,1,0:T(8,128)} fusion(bf16[8,4,128,128]{3,2,1,0:T(8,128)(2,1)} %multiply_convert_fusion.1, bf16[8,128,4,128]{1,3,2,0:T(8,128)(2,1)S(1)} %bitcast.353), kind=kOutput, calls=%fused_computation.186 | convolution fusion | flops 134217728 | bytes 4194304 | tf_op jit(solution)/shard_map/nhts,nshd->nthd/dot_general | solution.py:53
  189.4 24.3 %all-gather.10.cloned.1.call-done = f32[4,4,128,128]{3,2,1,0:T(8,128)} async-done(((f32[1,4,128,128]{3,2,1,0:T(8,128)}), f32[4,4,128,128]{3,2,1,0:T(8,128)}) %all-gather.10.cloned.1.call-update) | async-done | bytes 1048592 | tf_op jit(solution)/shard_map/all_gather | solution.py:32
  213.7 2.4 fusion.56
  216.2 1.9 fusion.23
  218.1 3.0 %fusion.13 = bf16[8,128,4,128]{1,3,2,0:T(8,128)(2,1)} fusion(f32[8,4,128,128]{2,3,1,0:T(8,128)S(1)} %copy-done.7, f32[8,4,128,128]{3,2,1,0:T(8,128)S(1)} %fusion.23, bf16[8,128,4,128]{1,3,2,0:T(8,128)(2,1)} %bitcast.11, f32[8,4,128,128]{3,2,1,0:T(8,128)S(1)} %copy-done.4, f32[4,128,128]{2,1,0:T(8,128)S(1)} %fusion.56, f32[8,4]{1,0:T(8,128)S(1)} %exp.200, ...), kind=kOutput, calls=%fused_computation.24 | convolution fusion | flops 139460608 | bytes 8667264 | tf_op jit(solution)/shard_map/nthb,nhab->ntha/dot_general | solution.py:53
  221.1 5.9 %all-to-all-start.4 = ((bf16[8,128,512]{1,2,0:T(8,128)(2,1)}), bf16[8,128,512]{1,2,0:T(8,128)(2,1)}, u32[]{:S(2)}, u32[]{:S(2)}) async-start(bf16[8,128,512]{1,2,0:T(8,128)(2,1)} %bitcast.371), calls=%async_computation.4 | async-start | bytes 2097152 | tf_op jit(solution)/shard_map/all_to_all | solution.py:207
  227.0 15.3 %all-gather.12.cloned.1.call-done = f32[4,4,128,128]{3,2,1,0:T(8,128)} async-done(((f32[1,4,128,128]{3,2,1,0:T(8,128)}), f32[4,4,128,128]{3,2,1,0:T(8,128)}) %all-gather.12.cloned.1.call-update) | async-done | bytes 1048592 | tf_op jit(solution)/shard_map/all_gather | solution.py:32
  242.3 2.3 fusion.44
  246.7 1.5 fusion.11
  248.2 5.9 %all-to-all-start.6 = ((bf16[8,128,512]{1,2,0:T(8,128)(2,1)}), bf16[8,128,512]{1,2,0:T(8,128)(2,1)}, u32[]{:S(2)}, u32[]{:S(2)}) async-start(bf16[8,128,512]{1,2,0:T(8,128)(2,1)} %bitcast.367), calls=%async_computation.6 | async-start | bytes 2097152 | tf_op jit(solution)/shard_map/all_to_all | solution.py:208
  254.1 4.0 %fusion.22 = f32[8,4,128,128]{3,2,1,0:T(8,128)} fusion(bf16[8,128,4,128]{1,3,2,0:T(8,128)(2,1)} %bitcast.11, bf16[8,128,4,128]{1,3,2,0:T(8,128)(2,1)} %bitcast.364, bf16[8,128,4,128]{1,3,2,0:T(8,128)(2,1)S(1)} %bitcast.354, f32[8,4,128]{2,1,0:T(4,128)S(1)} %copy.65, pred[128,128]{1,0:T(8,128)(4,1)S(1)} %iota_compare_fusion), kind=kOutput, calls=%fused_computation.44 | convolution fusion | flops 271056896 | bytes 5275648 | tf_op jit(solution)/shard_map/nhts,nthd->nshd/dot_general | solution.py:53
  259.7 1.8 fusion.9
  261.5 7.8 %all-to-all-done.6 = bf16[8,128,512]{1,2,0:T(8,128)(2,1)} async-done(((bf16[8,128,512]{1,2,0:T(8,128)(2,1)}), bf16[8,128,512]{1,2,0:T(8,128)(2,1)}, u32[]{:S(2)}, u32[]{:S(2)}) %all-to-all-start.6) | async-done | bytes 1048608 | tf_op jit(solution)/shard_map/all_to_all | solution.py:208
  269.3 4.3 %all-to-all-start.7 = ((bf16[8,128,512]{1,2,0:T(8,128)(2,1)}), bf16[8,128,512]{1,2,0:T(8,128)(2,1)S(1)}, u32[]{:S(2)}, u32[]{:S(2)}) async-start(bf16[8,128,512]{1,2,0:T(8,128)(2,1)} %bitcast.372), calls=%async_computation.7 | async-start | bytes 2097152 | tf_op jit(solution)/shard_map/all_to_all | solution.py:209
  273.6 2.3 copy.120
  275.9 2.3 copy.122
  278.2 10.6 %all-to-all-done.7 = bf16[8,128,512]{1,2,0:T(8,128)(2,1)S(1)} async-done(((bf16[8,128,512]{1,2,0:T(8,128)(2,1)}), bf16[8,128,512]{1,2,0:T(8,128)(2,1)S(1)}, u32[]{:S(2)}, u32[]{:S(2)}) %all-to-all-start.7) | async-done | bytes 1048608 | tf_op jit(solution)/shard_map/all_to_all | solution.py:209
  288.8 1.3 copy.123
  (134 shorter events, 19.2 us)
Async XLA Ops:
  7.2 14.0 %all-to-all-start = ((bf16[128,8,4]{0,2,1:T(4,128)(2,1)}), bf16[128,8,4]{0,2,1:T(4,128)(2,1)S(1)}, u32[]{:S(2)}, u32[]{:S(2)}) async-start(bf16[128,8,4]{0,2,1:T(4,128)(2,1)} %bitcast.374), calls=%async_computation | async-start | bytes 16384 | tf_op jit(solution)/shard_map/all_to_all | solution.py:177
  13.6 2.5 copy-start.12
  17.5 2.4 copy-start.13
  21.2 19.9 %all-to-all-start.2 = ((bf16[128,8,512]{0,2,1:T(8,128)(2,1)}), bf16[128,8,512]{0,2,1:T(8,128)(2,1)S(1)}, u32[]{:S(2)}, u32[]{:S(2)}) async-start(bf16[128,8,512]{0,2,1:T(8,128)(2,1)} %bitcast.12), calls=%async_computation.2 | async-start | bytes 2097152 | tf_op jit(solution)/shard_map/all_to_all | solution.py:175
  26.1 15.0 %copy-start.11 = (bf16[8,128,512]{1,2,0:T(8,128)(2,1)}, bf16[8,128,512]{1,2,0:T(8,128)(2,1)S(1)}, u32[]{:S(2)}) copy-start(bf16[8,128,512]{1,2,0:T(8,128)(2,1)S(1)} %bitcast_dynamic-update-slice_fusion.4) | copy-start | bytes 3145732
  41.1 28.9 %copy-start.2 = (bf16[128,8,512]{0,2,1:T(8,128)(2,1)}, bf16[128,8,512]{0,2,1:T(8,128)(2,1)S(1)}, u32[]{:S(2)}) copy-start(bf16[128,8,512]{0,2,1:T(8,128)(2,1)S(1)} %all-to-all-done.2) | copy-start | bytes 3145732
  41.1 19.5 %all-to-all-start.3 = ((bf16[128,8,512]{0,2,1:T(8,128)(2,1)}), bf16[128,8,512]{0,2,1:T(8,128)(2,1)S(1)}, u32[]{:S(2)}, u32[]{:S(2)}) async-start(bf16[128,8,512]{0,2,1:T(8,128)(2,1)} %bitcast.369), calls=%async_computation.3 | async-start | bytes 2097152 | tf_op jit(solution)/shard_map/all_to_all | solution.py:174
  49.0 18.9 %copy-start.8 = (f32[8,128,4]{2,0,1:T(8,128)}, f32[8,128,4]{2,0,1:T(8,128)S(1)}, u32[]{:S(2)}) copy-start(f32[8,128,4]{2,0,1:T(8,128)S(1)} %fusion.90) | copy-start | bytes 49156
  60.5 20.2 %all-to-all-start.1 = ((bf16[8,128,512]{1,2,0:T(8,128)(2,1)}), bf16[8,128,512]{1,2,0:T(8,128)(2,1)}, u32[]{:S(2)}, u32[]{:S(2)}) async-start(bf16[8,128,512]{1,2,0:T(8,128)(2,1)} %bitcast_dynamic-update-slice_fusion.2), calls=%async_computation.1 | async-start | bytes 2097152 | tf_op jit(solution)/shard_map/all_to_all | solution.py:14
  80.8 21.5 %all-to-all-start.5 = ((bf16[128,8,512]{0,2,1:T(8,128)(2,1)}), bf16[128,8,512]{0,2,1:T(8,128)(2,1)S(1)}, u32[]{:S(2)}, u32[]{:S(2)}) async-start(bf16[128,8,512]{0,2,1:T(8,128)(2,1)} %bitcast.368), calls=%async_computation.5 | async-start | bytes 2097152 | tf_op jit(solution)/shard_map/all_to_all | solution.py:173
  85.1 57.0 %all-gather.14.cloned.1.call-start = ((), (), s32[]{:S(2)}) async-start(), calls=%async_computation.10 | async-start | bytes 2359296 | tf_op jit(solution)/shard_map/all_gather | solution.py:32
  101.5 0.7 copy-start.1
  102.3 81.2 %all-gather.16.cloned.1.call-start = ((), (), s32[]{:S(2)}) async-start(), calls=%async_computation.11 | async-start | bytes 2359296 | tf_op jit(solution)/shard_map/all_gather | solution.py:32
  102.3 2.5 copy-start.5
  108.5 10.1 %copy-start.14 = (u32[256]{0:T(256)S(1)}, u32[256]{0:T(256)}, u32[]{:S(2)}) copy-start(u32[256]{0:T(256)} %constant.92) | copy-start | bytes 3076
  117.7 0.7 copy-start
  118.5 95.3 %all-gather.10.cloned.1.call-start = ((), (), s32[]{:S(2)}) async-start(), calls=%async_computation.8 | async-start | bytes 1310720 | tf_op jit(solution)/shard_map/all_gather | solution.py:32
  144.6 97.7 %all-gather.12.cloned.1.call-start = ((), (), s32[]{:S(2)}) async-start(), calls=%async_computation.9 | async-start | bytes 1310720 | tf_op jit(solution)/shard_map/all_gather | solution.py:32
  213.7 2.5 copy-start.4
  216.2 1.9 copy-start.7
  221.1 27.1 %all-to-all-start.4 = ((bf16[8,128,512]{1,2,0:T(8,128)(2,1)}), bf16[8,128,512]{1,2,0:T(8,128)(2,1)}, u32[]{:S(2)}, u32[]{:S(2)}) async-start(bf16[8,128,512]{1,2,0:T(8,128)(2,1)} %bitcast.371), calls=%async_computation.4 | async-start | bytes 2097152 | tf_op jit(solution)/shard_map/all_to_all | solution.py:207
  242.3 2.3 copy-start.3
  245.2 1.2 copy-start.6
  245.2 1.5 copy-start.9
  248.2 21.1 %all-to-all-start.6 = ((bf16[8,128,512]{1,2,0:T(8,128)(2,1)}), bf16[8,128,512]{1,2,0:T(8,128)(2,1)}, u32[]{:S(2)}, u32[]{:S(2)}) async-start(bf16[8,128,512]{1,2,0:T(8,128)(2,1)} %bitcast.367), calls=%async_computation.6 | async-start | bytes 2097152 | tf_op jit(solution)/shard_map/all_to_all | solution.py:208
  258.1 1.6 copy-start.10
  269.3 19.4 %all-to-all-start.7 = ((bf16[8,128,512]{1,2,0:T(8,128)(2,1)}), bf16[8,128,512]{1,2,0:T(8,128)(2,1)S(1)}, u32[]{:S(2)}, u32[]{:S(2)}) async-start(bf16[8,128,512]{1,2,0:T(8,128)(2,1)} %bitcast.372), calls=%async_computation.7 | async-start | bytes 2097152 | tf_op jit(solution)/shard_map/all_to_all | solution.py:209
Sparse Core Ops, SparseCore 0:
  102.4 39.6 all-gather.13
  143.9 39.5 all-gather.15
  185.9 27.8 all-gather.9
  215.4 26.8 all-gather.11
